TPU v7x, 128 devices: a whole 4x4x4 slice. The times are simulated.
128 devices in a mesh: chan: 4 (over z_lo, core), blk: 32 (over z_hi, y, x).
Axes of the slice: x: 4, y: 4, z: 4 (z_hi: 2, z_lo: 2; z = z_hi * 2 + z_lo), core: 2. Of those that a mesh axis runs over, the one named last changes fastest.
Arguments:
- voltages: bfloat16 [256, 262144], P('blk', 'chan'), may hold values from -6 to 6
- fir_taps: float32 [8, 4096], replicated, may hold values from -2.1 to 2.1
Outputs:
- visibilities: float32 [2, 256, 256, 2048], P(None, 'blk', None, 'chan')
All inputs are finite; a program needn't handle non-finite values.
Results may differ from a plain program's by a relative error of at most 0.0036.
Values may be sent and summed in bfloat16 or wider, within the bound.
No kernel may reach another device: no remote copies, remote signals or barrier semaphores. Data moves between devices by JAX's collectives and lax.ppermute only.
A program may use at most 192 MiB of HBM per device.

v0:
```python
import math
import jax
import jax.numpy as jnp
from jax import lax
from jax.experimental.layout import Layout, with_layout_constraint
from jax.sharding import PartitionSpec as P

TAPS = 8
L = 4096
C = 2048


def shifted(value, axis, steps):
    count = lax.axis_size(axis)
    leading, last = (max(0, -steps), min(count, count - steps))
    return lax.ppermute(value, axis, [(source, source + steps) for source in range(leading, last)])


def dft_table(first_channel, channel_count, length):
    channel_ids = first_channel + jnp.arange(channel_count, dtype=jnp.int32)
    sample_ids = jnp.arange(length, dtype=jnp.int32)
    phase_index = sample_ids[:, None] * channel_ids[None, :] % length
    angles = phase_index.astype(jnp.float32) * (2.0 * math.pi / length)
    normaliser = 1.0 / math.sqrt(length)
    return jnp.concatenate([jnp.cos(angles) * normaliser, -jnp.sin(angles) * normaliser], axis=1)


def correlate(own_block, every_block, inverse_count):
    real_part, imag_part = (own_block[:, 0], own_block[:, 1])
    paired = jnp.stack(
        [jnp.stack([real_part, imag_part], axis=1), jnp.stack([imag_part, -real_part], axis=1)]
    )
    products = jnp.einsum(
        "riptc,jptc->rijc", paired, every_block, preferred_element_type=jnp.float32
    )
    return products * inverse_count


def on_device(voltages, fir_taps):
    feed_count = voltages.shape[0]
    frame_count = voltages.shape[1] // L
    own_frames = voltages.reshape(feed_count, frame_count, L)
    last_frames = own_frames[:, frame_count - (TAPS - 1) :, :]
    earlier = shifted(last_frames, "chan", 1)
    extended = jnp.concatenate([earlier, own_frames], axis=1)
    filtered = jnp.zeros((feed_count, frame_count, L), jnp.float32)
    for tap_index in range(TAPS):
        filtered = filtered + fir_taps[tap_index][None, None, :] * extended[
            :, tap_index : tap_index + frame_count, :
        ].astype(jnp.float32)
    frame_rows = filtered.reshape(feed_count * frame_count, L)
    block_width = min(C, 512)
    pieces = []
    for first_channel in range(0, C, block_width):
        cos_sin_table = dft_table(first_channel, block_width, L)
        product = jnp.dot(
            frame_rows,
            cos_sin_table,
            precision=lax.Precision.HIGHEST,
            preferred_element_type=jnp.float32,
        )
        pieces.append(product.reshape(feed_count * frame_count, 2, block_width))
    spectra = (
        jnp.concatenate(pieces, axis=2).astype(jnp.bfloat16).reshape(feed_count, frame_count, 2, C)
    )
    own_block = lax.all_to_all(spectra, "chan", split_axis=3, concat_axis=1, tiled=True)
    inverse_count = 1.0 / own_block.shape[1]
    own_block = own_block.transpose(0, 2, 1, 3)
    row_major = Layout(major_to_minor=tuple(range(own_block.ndim + 1)))
    local = with_layout_constraint(own_block[None], row_major)
    gathered = with_layout_constraint(lax.all_gather(local, "blk", axis=0, tiled=True), row_major)
    every_block = gathered.reshape((-1,) + own_block.shape[1:])
    return correlate(own_block, every_block, inverse_count)


def solution(mesh):
    placed = (P("blk", "chan"), P())
    return jax.shard_map(
        on_device,
        mesh=mesh,
        in_specs=placed,
        out_specs=P(None, "blk", None, "chan"),
        check_vma=False,
    )
```

profile of v0, /device:TPU:0, one launch (start us, length us, event | category | flops | bytes accessed | tf_op | source)
XLA Modules:
  0.0 691.3 jit_solution(8309814555249872896)
XLA Ops:
  6.5 0.0 all-gather.2.cloned.1.call-start
  6.5 1.8 copy.10
  8.3 0.1 slice.73
  8.5 2.1 collective-permute-start
  10.6 0.0 copy-start.6
  10.6 33.0 %negate_multiply_fusion.3 = (f32[4096,512]{0,1:T(8,128)S(1)}, f32[4096,512]{0,1:T(8,128)S(1)}) fusion(), kind=kLoop, calls=%fused_computation.42 | loop fusion | flops 35651584 | bytes 16777216 | tf_op jit(solution)/shard_map/mul | solution.py:25
  43.6 0.0 copy-done.6
  43.6 0.1 fusion.52
  43.7 33.8 %cosine_multiply_fusion = (f32[4096,512]{0,1:T(8,128)S(1)}, f32[4096,512]{0,1:T(8,128)S(1)}) fusion(s32[512]{0:T(512)S(1)} %iota_add_fusion), kind=kLoop, calls=%fused_computation.31 | loop fusion | flops 35651584 | bytes 16779264 | tf_op jit(solution)/shard_map/mul | solution.py:25
  77.5 37.2 %cosine_multiply_fusion.1 = (f32[4096,512]{0,1:T(8,128)}, f32[4096,512]{0,1:T(8,128)}) fusion(s32[512]{0:T(512)S(1)} %iota_add_fusion.1), kind=kLoop, calls=%fused_computation.35 | loop fusion | flops 35651584 | bytes 16779264 | tf_op jit(solution)/shard_map/mul | solution.py:25
  114.7 37.2 %cosine_multiply_fusion.2 = (f32[4096,512]{0,1:T(8,128)}, f32[4096,512]{0,1:T(8,128)}) fusion(s32[512]{0:T(512)S(1)} %iota_add_fusion.2), kind=kLoop, calls=%fused_computation.39 | loop fusion | flops 35651584 | bytes 16779264 | tf_op jit(solution)/shard_map/mul | solution.py:25
  151.9 6.4 pad_maximum_fusion.3
  158.3 0.0 copy-start
  158.3 0.0 copy-start.1
  158.3 13.7 %pad_maximum_fusion.2 = f32[4096,1024]{0,1:T(8,128)} fusion(f32[4096,512]{0,1:T(8,128)} %get-tuple-element.18, f32[4096,512]{0,1:T(8,128)} %get-tuple-element.17), kind=kLoop, calls=%fused_computation.2 | loop fusion | flops 4194304 | bytes 33554432 | tf_op jit(solution)/shard_map/concatenate | solution.py:25
  172.0 0.0 copy-done
  172.0 2.7 copy-done.1
  174.8 6.6 pad_maximum_fusion.1
  181.3 6.4 pad_maximum_fusion
  187.8 0.0 collective-permute-done
  187.8 0.0 slice-start
  187.8 5.6 multiply_add_fusion
  193.4 0.0 copy-start.2
  193.4 0.0 slice-start.1
  193.4 0.0 slice-start.2
  193.4 0.0 slice-start.3
  193.5 22.5 %fusion.42 = bf16[8,16,2,512]{3,1,2,0:T(8,128)(2,1)} fusion(f32[2,512,4096,1]{2,1,0,3:T(8,128)} %bitcast.79, f32[8,16,4096]{2,1,0:T(8,128)S(1)} %multiply_add_fusion), kind=kOutput, calls=%fused_computation.75 | convolution fusion | flops 6442582016 | bytes 19136512 | tf_op jit(solution)/shard_map/dot_general | solution.py:56
  215.9 0.0 copy-done.2
  216.0 0.0 slice-done
  216.0 0.0 slice-done.1
  216.0 0.0 slice-done.2
  216.0 0.0 slice-done.3
  216.0 0.0 copy-start.3
  216.0 0.0 slice-start.4
  216.0 0.0 slice-start.5
  216.0 20.0 %fusion.39 = bf16[8,16,2,512]{3,1,2,0:T(8,128)(2,1)} fusion(f32[2,512,4096,1]{2,1,0,3:T(8,128)S(1)} %bitcast.82, f32[8,16,4096]{2,1,0:T(8,128)} %copy-done.2), kind=kOutput, calls=%fused_computation.74 | convolution fusion | flops 6442582016 | bytes 19136512 | tf_op jit(solution)/shard_map/dot_general | solution.py:56
  236.0 0.0 copy-done.3
  236.0 0.0 slice-start.6
  236.0 0.0 slice-start.7
  236.0 20.8 %fusion.36 = bf16[8,16,2,512]{3,1,2,0:T(8,128)(2,1)S(1)} fusion(f32[2,512,4096,1]{2,1,0,3:T(8,128)} %bitcast.83, f32[8,16,4096]{2,1,0:T(8,128)S(1)} %copy-done.3), kind=kOutput, calls=%fused_computation.73 | convolution fusion | flops 6442582016 | bytes 19136512 | tf_op jit(solution)/shard_map/dot_general | solution.py:56
  256.8 0.0 slice-done.4
  256.8 0.0 slice-done.5
  256.8 0.0 slice-done.6
  256.8 0.0 slice-done.7
  256.8 0.0 copy-start.4
  256.8 0.0 copy-start.5
  256.9 17.6 %fusion.33 = bf16[8,16,2,512]{3,1,2,0:T(8,128)(2,1)S(1)} fusion(f32[2,512,4096,1]{2,1,0,3:T(8,128)S(1)} %bitcast.86, f32[8,16,4096]{2,1,0:T(8,128)S(1)} %copy-done.3), kind=kOutput, calls=%fused_computation.72 | convolution fusion | flops 6442582016 | bytes 19136512 | tf_op jit(solution)/shard_map/dot_general | solution.py:56
  274.5 0.0 copy-done.4
  274.5 0.0 copy-done.5
  274.5 0.1 pad_maximum_fusion.6
  274.6 14.3 %copy.13 = bf16[8,16,2,2048]{1,2,0,3:T(2,128)(2,1)} copy(bf16[8,16,2,2048]{3,1,2,0:T(8,128)(2,1)S(1)} %pad_maximum_fusion.6) | data formatting | bytes 2097152 | tf_op jit(solution)/shard_map/concatenate | solution.py:64
  288.9 10.2 %reshape.57 = bf16[4,2,65536]{2,1,0:T(2,128)(2,1)S(1)} reshape(bf16[2048,8,2,16]{3,2,1,0:T(2,128)(2,1)} %bitcast.76) | data formatting | bytes 2097152
  299.2 17.5 %all_to_all.18 = bf16[4,2,65536]{2,1,0:T(2,128)(2,1)S(1)} all-to-all(bf16[4,2,65536]{2,1,0:T(2,128)(2,1)S(1)} %reshape.57), channel_id=1, replica_groups=mesh['chan'=4,'blk'=32] {'chan'}, dimensions={0} | all-to-all | bytes 2097152 | tf_op jit(solution)/shard_map/all_to_all | solution.py:66
  316.6 7.1 %reshape.58 = bf16[2048,8,2,16]{3,2,1,0:T(2,128)(2,1)} reshape(bf16[4,2,65536]{2,1,0:T(2,128)(2,1)S(1)} %all_to_all.18) | data formatting | bytes 2097152
  323.7 19.3 %copy.14 = bf16[8,16,2,4,512]{4,1,3,2,0:T(8,128)(2,1)} copy(bf16[8,16,2,4,512]{1,2,0,4,3:T(2,128)(2,1)} %bitcast.77) | data formatting | bytes 2097152 | tf_op jit(solution)/shard_map/all_to_all | solution.py:66
  343.1 0.0 all-gather.2.cloned.1.call-update
  343.1 1.3 fusion.51
  344.4 0.1 maximum_bitcast_fusion
  344.5 1.4 pad_maximum_fusion.4
  345.9 6.6 copy.16
  352.5 253.8 %all-gather.2.cloned.1.call-done = bf16[32,8,2,64,512]{4,3,2,1,0:T(8,128)(2,1)} async-done(((bf16[1,8,2,64,512]{4,3,2,1,0:T(8,128)(2,1)}), bf16[32,8,2,64,512]{4,3,2,1,0:T(8,128)(2,1)}) %all-gather.2.cloned.1.call-update) | async-done | bytes 33554448 | tf_op jit(solution)/shard_map/all_gather | solution.py:71
  606.3 50.8 %copy.19 = bf16[256,2,64,512,1]{0,2,1,4,3:T(8,128)(2,1)} copy(bf16[256,2,64,512,1]{3,2,1,0,4:T(8,128)(2,1)} %bitcast.78) | data formatting | bytes 67108864 | tf_op jit(solution)/shard_map/reshape | solution.py:72
  657.0 17.2 %fusion.12 = f32[2,8,256,512]{2,1,0,3:T(8,128)} fusion(bf16[256,2,64,512,1]{0,2,1,4,3:T(8,128)(2,1)} %copy.19, bf16[2,8,2,64,512]{3,1,2,0,4:T(8,128)(2,1)} %copy.16), kind=kOutput, calls=%fused_computation.29 | convolution fusion | flops 538968064 | bytes 44040192 | tf_op jit(solution)/shard_map/riptc,jptc->rijc/dot_general | solution.py:33
  674.2 9.9 %copy.17 = f32[2,8,256,512]{3,2,1,0:T(8,128)} copy(f32[2,8,256,512]{2,1,0,3:T(8,128)} %fusion.12) | data formatting | bytes 16777216 | tf_op jit(solution)/shard_map/mul | solution.py:36
  (5 shorter events, 0.0 us)
Async XLA Ops:
  6.5 599.7 %all-gather.2.cloned.1.call-start = ((), (), s32[]{:S(2)}) async-start(), calls=%async_computation.1 | async-start | bytes 34603008 | tf_op jit(solution)/shard_map/all_gather | solution.py:71
  8.5 179.3 %collective-permute-start = (bf16[8,7,4096]{2,1,0:T(8,128)(2,1)S(1)}, bf16[8,7,4096]{2,1,0:T(8,128)(2,1)}, u32[]{:S(2)}, u32[]{:S(2)}) collective-permute-start(bf16[8,7,4096]{2,1,0:T(8,128)(2,1)S(1)} %slice.73), channel_id=1, source_target_pairs={{0,32},{32,64},{64,96},{1,33},{33,65},{65,97},{2,34},{34,66},{66,9... | collective-permute-start | bytes 1376264 | tf_op jit(solution)/shard_map/ppermute | solution.py:16
  10.6 33.0 %copy-start.6 = (f32[8,4096]{1,0:T(8,128)S(1)}, f32[8,4096]{1,0:T(8,128)}, u32[]{:S(2)}) copy-start(f32[8,4096]{1,0:T(8,128)} %param.3) | copy-start | bytes 393220
  158.3 13.7 %copy-start = (f32[4096,512]{0,1:T(8,128)S(1)}, f32[4096,512]{0,1:T(8,128)}, u32[]{:S(2)}) copy-start(f32[4096,512]{0,1:T(8,128)} %get-tuple-element.15) | copy-start | bytes 25165828
  158.3 16.5 %copy-start.1 = (f32[4096,512]{0,1:T(8,128)S(1)}, f32[4096,512]{0,1:T(8,128)}, u32[]{:S(2)}) copy-start(f32[4096,512]{0,1:T(8,128)} %get-tuple-element.16) | copy-start | bytes 25165828
  187.8 28.2 %slice-start = ((s8[16777216]{0:T(1024)(128)(4,1)}), s8[4194304]{0:T(1024)(128)(4,1)S(1)}, s32[]{:S(2)}) async-start(s8[16777216]{0:T(1024)(128)(4,1)} %bitcast.80), calls=%async_computation.2 | async-start | bytes 8388608
  193.4 22.5 %copy-start.2 = (f32[8,16,4096]{2,1,0:T(8,128)}, f32[8,16,4096]{2,1,0:T(8,128)S(1)}, u32[]{:S(2)}) copy-start(f32[8,16,4096]{2,1,0:T(8,128)S(1)} %multiply_add_fusion) | copy-start | bytes 6291460
  193.4 22.5 %slice-start.1 = ((s8[16777216]{0:T(1024)(128)(4,1)}), s8[4194304]{0:T(1024)(128)(4,1)S(1)}, s32[]{:S(2)}) async-start(s8[16777216]{0:T(1024)(128)(4,1)} %bitcast.80), calls=%async_computation.3 | async-start | bytes 8388608
  193.4 22.5 %slice-start.2 = ((s8[16777216]{0:T(1024)(128)(4,1)}), s8[4194304]{0:T(1024)(128)(4,1)S(1)}, s32[]{:S(2)}) async-start(s8[16777216]{0:T(1024)(128)(4,1)} %bitcast.80), calls=%async_computation.4 | async-start | bytes 8388608
  193.4 22.5 %slice-start.3 = ((s8[16777216]{0:T(1024)(128)(4,1)}), s8[4194304]{0:T(1024)(128)(4,1)S(1)}, s32[]{:S(2)}) async-start(s8[16777216]{0:T(1024)(128)(4,1)} %bitcast.80), calls=%async_computation.5 | async-start | bytes 8388608
  216.0 20.0 %copy-start.3 = (f32[8,16,4096]{2,1,0:T(8,128)S(1)}, f32[8,16,4096]{2,1,0:T(8,128)}, u32[]{:S(2)}) copy-start(f32[8,16,4096]{2,1,0:T(8,128)} %copy-done.2) | copy-start | bytes 6291460
  216.0 40.8 %slice-start.4 = ((s8[16777216]{0:T(1024)(128)(4,1)}), s8[4194304]{0:T(1024)(128)(4,1)S(1)}, s32[]{:S(2)}) async-start(s8[16777216]{0:T(1024)(128)(4,1)} %bitcast.84), calls=%async_computation.6 | async-start | bytes 8388608
  216.0 40.8 %slice-start.5 = ((s8[16777216]{0:T(1024)(128)(4,1)}), s8[4194304]{0:T(1024)(128)(4,1)S(1)}, s32[]{:S(2)}) async-start(s8[16777216]{0:T(1024)(128)(4,1)} %bitcast.84), calls=%async_computation.7 | async-start | bytes 8388608
  236.0 20.8 %slice-start.6 = ((s8[16777216]{0:T(1024)(128)(4,1)}), s8[4194304]{0:T(1024)(128)(4,1)S(1)}, s32[]{:S(2)}) async-start(s8[16777216]{0:T(1024)(128)(4,1)} %bitcast.84), calls=%async_computation.8 | async-start | bytes 8388608
  236.0 20.8 %slice-start.7 = ((s8[16777216]{0:T(1024)(128)(4,1)}), s8[4194304]{0:T(1024)(128)(4,1)S(1)}, s32[]{:S(2)}) async-start(s8[16777216]{0:T(1024)(128)(4,1)} %bitcast.84), calls=%async_computation.9 | async-start | bytes 8388608
  256.8 17.6 %copy-start.4 = (bf16[8,16,2,512]{3,1,2,0:T(8,128)(2,1)S(1)}, bf16[8,16,2,512]{3,1,2,0:T(8,128)(2,1)}, u32[]{:S(2)}) copy-start(bf16[8,16,2,512]{3,1,2,0:T(8,128)(2,1)} %fusion.42) | copy-start | bytes 786436
  256.8 17.6 %copy-start.5 = (bf16[8,16,2,512]{3,1,2,0:T(8,128)(2,1)S(1)}, bf16[8,16,2,512]{3,1,2,0:T(8,128)(2,1)}, u32[]{:S(2)}) copy-start(bf16[8,16,2,512]{3,1,2,0:T(8,128)(2,1)} %fusion.39) | copy-start | bytes 786436
Sparse Core Ops, SparseCore 0:
  343.2 263.0 all-gather.1
where the time goes:
time: 701 us; the launch traced here: 691 us
  waiting for transfers between devices  254 us (36%)
  other arithmetic  183 us (26%)
  local copies, waits for them, and re-layouts  123 us (18%)
  matrix products  98 us (14%)
  blocking collectives  17.5 us (2%)
  between operations  14.1 us (2%)
    all_gather x1, waiting for transfers between devices, on_device(): lax.all_gather(local, 'blk', axis=0, tiled=True)  254 us
    mul x3, other arithmetic, dft_table(): jnp.cos(angles) * normaliser  108 us
    dot_general x4, matrix products, on_device(): jnp.dot(frame_rows, cos_sin_table, precision=lax.Precision.HIGHEST, prefe...  80.8 us
    reshape x1, local copies, waits for them, and re-layouts, on_device(): every_block = gathered.reshape((-1,) + own_block.shape[1:])  50.8 us
    concatenate x4, other arithmetic, dft_table(): jnp.concatenate([jnp.cos(angles) * normaliser, -jnp.sin(angles) * normali...  33.1 us
    mul x1, other arithmetic, dft_table(): -jnp.sin(angles) * normaliser  33 us
    unnamed x32, local copies, waits for them, and re-layouts  20.1 us
    all_to_all x1, local copies, waits for them, and re-layouts, on_device(): lax.all_to_all(spectra, 'chan', split_axis=3, concat_axis=1, tiled=True)  19.3 us
  transfers between devices with their start and end apart: 2, of which 1 were waited for; matrix products, arithmetic and copies ran while one was open for 27% of the time, Pallas kernels for 0%

commit v1 on v0

--- a/solution.py
+++ b/solution.py
@@ -63,7 +63,10 @@
     spectra = (
         jnp.concatenate(pieces, axis=2).astype(jnp.bfloat16).reshape(feed_count, frame_count, 2, C)
     )
-    own_block = lax.all_to_all(spectra, "chan", split_axis=3, concat_axis=1, tiled=True)
+    own_block = jnp.concatenate(
+        lax.all_to_all(jnp.stack(jnp.split(spectra, lax.axis_size("chan"), axis=3)), "chan", 0, 0),
+        axis=1,
+    )
     inverse_count = 1.0 / own_block.shape[1]
     own_block = own_block.transpose(0, 2, 1, 3)
     row_major = Layout(major_to_minor=tuple(range(own_block.ndim + 1)))

time: 701 us -> 650 us (0.927)
  local copies, waits for them, and re-layouts: 123 us -> 73.2 us
    all_to_all x1 -> x0, local copies, waits for them, and re-layouts: 19.3 us -> none  [on_device(): lax.all_to_all(spectra, 'chan', split_axis=3, concat_axis=1, tiled=True)]
    unnamed x32 -> x30, local copies, waits for them, and re-layouts: 20.1 us -> 2.81 us
    concatenate x1 -> x0, local copies, waits for them, and re-layouts: 14.3 us -> none  [on_device(): jnp.concatenate(pieces, axis=2).astype(jnp.bfloat16)]
  transfers between devices with their start and end apart: 2 -> 2, of which waited for: 1 -> 1; matrix products, arithmetic and copies ran while one was open for 27% -> 29% of each run, Pallas kernels for 0% -> 0%
where the time goes in v1:
time: 650 us; the launch traced here: 641 us
  waiting for transfers between devices  254 us (39%)
  other arithmetic  183 us (28%)
  matrix products  98 us (15%)
  local copies, waits for them, and re-layouts  73.2 us (11%)
  blocking collectives  17.5 us (3%)
  between operations  13.9 us (2%)
    all_gather x1, waiting for transfers between devices, on_device(): lax.all_gather(local, 'blk', axis=0, tiled=True)  254 us
    mul x3, other arithmetic, dft_table(): jnp.cos(angles) * normaliser  108 us
    dot_general x4, matrix products, on_device(): jnp.dot(frame_rows, cos_sin_table, precision=lax.Precision.HIGHEST, prefe...  80.8 us
    reshape x1, local copies, waits for them, and re-layouts, on_device(): every_block = gathered.reshape((-1,) + own_block.shape[1:])  50.8 us
    concatenate x4, other arithmetic, dft_table(): jnp.concatenate([jnp.cos(angles) * normaliser, -jnp.sin(angles) * normali...  33.4 us
    mul x1, other arithmetic, dft_table(): -jnp.sin(angles) * normaliser  33 us
    all_to_all x1, blocking collectives, on_device(): lax.all_to_all(jnp.stack(jnp.split(spectra, lax.axis_size('chan'), axis=3...  17.5 us
    dot_general x1, matrix products, correlate(): jnp.einsum('riptc,jptc->rijc', paired, every_block, preferred_element_typ...  17.2 us
  transfers between devices with their start and end apart: 2, of which 1 were waited for; matrix products, arithmetic and copies ran while one was open for 29% of the time, Pallas kernels for 0%

profile of v1, /device:TPU:0, one launch (start us, length us, event | category | flops | bytes accessed | tf_op | source)
XLA Modules:
  0.0 641.4 jit_solution(15346167007774536682)
XLA Ops:
  6.5 0.0 all-gather.2.cloned.1.call-start
  6.5 1.8 copy.10
  8.3 0.1 slice.73
  8.5 2.1 collective-permute-start
  10.6 0.0 copy-start.6
  10.6 33.0 %negate_multiply_fusion.3 = (f32[4096,512]{0,1:T(8,128)S(1)}, f32[4096,512]{0,1:T(8,128)S(1)}) fusion(), kind=kLoop, calls=%fused_computation.42 | loop fusion | flops 35651584 | bytes 16777216 | tf_op jit(solution)/shard_map/mul | solution.py:25
  43.6 0.0 copy-done.6
  43.6 0.1 fusion.64
  43.7 33.6 %cosine_multiply_fusion = (f32[4096,512]{0,1:T(8,128)S(1)}, f32[4096,512]{0,1:T(8,128)S(1)}) fusion(s32[512]{0:T(512)S(1)} %iota_add_fusion), kind=kLoop, calls=%fused_computation.31 | loop fusion | flops 35651584 | bytes 16779264 | tf_op jit(solution)/shard_map/mul | solution.py:25
  77.3 37.2 %cosine_multiply_fusion.1 = (f32[4096,512]{0,1:T(8,128)}, f32[4096,512]{0,1:T(8,128)}) fusion(s32[512]{0:T(512)S(1)} %iota_add_fusion.1), kind=kLoop, calls=%fused_computation.35 | loop fusion | flops 35651584 | bytes 16779264 | tf_op jit(solution)/shard_map/mul | solution.py:25
  114.5 37.2 %cosine_multiply_fusion.2 = (f32[4096,512]{0,1:T(8,128)}, f32[4096,512]{0,1:T(8,128)}) fusion(s32[512]{0:T(512)S(1)} %iota_add_fusion.2), kind=kLoop, calls=%fused_computation.39 | loop fusion | flops 35651584 | bytes 16779264 | tf_op jit(solution)/shard_map/mul | solution.py:25
  151.8 6.4 pad_maximum_fusion.3
  158.1 0.0 copy-start
  158.1 0.0 copy-start.1
  158.1 13.7 %pad_maximum_fusion.2 = f32[4096,1024]{0,1:T(8,128)} fusion(f32[4096,512]{0,1:T(8,128)} %get-tuple-element.18, f32[4096,512]{0,1:T(8,128)} %get-tuple-element.17), kind=kLoop, calls=%fused_computation.2 | loop fusion | flops 4194304 | bytes 33554432 | tf_op jit(solution)/shard_map/concatenate | solution.py:25
  171.9 0.0 copy-done
  171.9 2.7 copy-done.1
  174.6 6.9 %pad_maximum_fusion.1 = f32[4096,1024]{0,1:T(8,128)} fusion(f32[4096,512]{0,1:T(8,128)S(1)} %copy-done.1, f32[4096,512]{0,1:T(8,128)S(1)} %copy-done), kind=kLoop, calls=%fused_computation.1 | loop fusion | flops 4194304 | bytes 33554432 | tf_op jit(solution)/shard_map/concatenate | solution.py:25
  181.5 6.4 %pad_maximum_fusion = f32[4096,1024]{0,1:T(8,128)} fusion(f32[4096,512]{0,1:T(8,128)S(1)} %get-tuple-element.21, f32[4096,512]{0,1:T(8,128)S(1)} %get-tuple-element.22), kind=kLoop, calls=%fused_computation | loop fusion | flops 4194304 | bytes 33554432 | tf_op jit(solution)/shard_map/concatenate | solution.py:25
  187.9 0.0 collective-permute-done
  187.9 0.0 slice-start
  187.9 5.6 multiply_add_fusion
  193.6 0.0 copy-start.2
  193.6 0.0 slice-start.1
  193.6 0.0 slice-start.2
  193.6 0.0 slice-start.3
  193.6 22.3 %fusion.45 = bf16[1,8,16,2,512]{4,2,3,1,0:T(8,128)(2,1)} fusion(f32[2,512,4096,1]{2,1,0,3:T(8,128)} %bitcast.89, f32[8,16,4096]{2,1,0:T(8,128)S(1)} %multiply_add_fusion), kind=kOutput, calls=%fused_computation.76 | convolution fusion | flops 6442582016 | bytes 19136512 | tf_op jit(solution)/shard_map/dot_general | solution.py:56
  215.9 0.0 copy-done.2
  215.9 0.0 slice-done
  215.9 0.0 slice-done.1
  215.9 0.0 slice-done.2
  215.9 0.0 slice-done.3
  216.0 0.0 copy-start.3
  216.0 0.0 slice-start.4
  216.0 0.0 slice-start.5
  216.0 20.2 %fusion.48 = bf16[1,8,16,2,512]{4,2,3,1,0:T(8,128)(2,1)} fusion(f32[2,512,4096,1]{2,1,0,3:T(8,128)S(1)} %bitcast.92, f32[8,16,4096]{2,1,0:T(8,128)} %copy-done.2), kind=kOutput, calls=%fused_computation.77 | convolution fusion | flops 6442582016 | bytes 19136512 | tf_op jit(solution)/shard_map/dot_general | solution.py:56
  236.2 0.0 copy-done.3
  236.2 0.0 slice-start.6
  236.2 0.0 slice-start.7
  236.2 20.8 %fusion.51 = bf16[1,8,16,2,512]{4,2,3,1,0:T(8,128)(2,1)S(1)} fusion(f32[2,512,4096,1]{2,1,0,3:T(8,128)} %bitcast.93, f32[8,16,4096]{2,1,0:T(8,128)S(1)} %copy-done.3), kind=kOutput, calls=%fused_computation.78 | convolution fusion | flops 6442582016 | bytes 19136512 | tf_op jit(solution)/shard_map/dot_general | solution.py:56
  257.0 0.0 slice-done.4
  257.0 0.0 slice-done.5
  257.0 0.0 slice-done.6
  257.0 0.0 slice-done.7
  257.0 0.0 copy-start.4
  257.0 0.0 copy-start.5
  257.0 17.6 %fusion.54 = bf16[1,8,16,2,512]{4,2,3,1,0:T(8,128)(2,1)S(1)} fusion(f32[2,512,4096,1]{2,1,0,3:T(8,128)S(1)} %bitcast.96, f32[8,16,4096]{2,1,0:T(8,128)S(1)} %copy-done.3), kind=kOutput, calls=%fused_computation.79 | convolution fusion | flops 6442582016 | bytes 19136512 | tf_op jit(solution)/shard_map/dot_general | solution.py:56
  274.6 0.0 copy-done.4
  274.6 0.0 copy-done.5
  274.6 0.1 pad_maximum_fusion.6
  274.8 17.5 %all_to_all.5 = bf16[4,8,16,2,512]{4,2,3,1,0:T(8,128)(2,1)S(1)} all-to-all(bf16[4,8,16,2,512]{4,2,3,1,0:T(8,128)(2,1)S(1)} %pad_maximum_fusion.6), channel_id=1, replica_groups=mesh['chan'=4,'blk'=32] {'chan'}, dimensions={0} | all-to-all | bytes 2097152 | tf_op jit(solution)/shard_map/all_to_all | solution.py:67
  292.2 1.1 copy.13
  293.3 0.0 all-gather.2.cloned.1.call-update
  293.3 1.3 fusion.63
  294.6 0.1 maximum_bitcast_fusion
  294.7 1.4 pad_maximum_fusion.4
  296.2 6.6 %copy.15 = bf16[2,8,2,64,512]{3,1,2,0,4:T(8,128)(2,1)} copy(bf16[2,8,2,64,512]{4,3,2,1,0:T(8,128)(2,1)S(1)} %pad_maximum_fusion.4) | data formatting | bytes 4194304 | tf_op jit(solution)/shard_map/stack | solution.py:30
  302.8 253.7 %all-gather.2.cloned.1.call-done = bf16[32,8,2,64,512]{4,3,2,1,0:T(8,128)(2,1)} async-done(((bf16[1,8,2,64,512]{4,3,2,1,0:T(8,128)(2,1)}), bf16[32,8,2,64,512]{4,3,2,1,0:T(8,128)(2,1)}) %all-gather.2.cloned.1.call-update) | async-done | bytes 33554448 | tf_op jit(solution)/shard_map/all_gather | solution.py:74
  556.5 50.8 %copy.18 = bf16[256,2,64,512,1]{0,2,1,4,3:T(8,128)(2,1)} copy(bf16[256,2,64,512,1]{3,2,1,0,4:T(8,128)(2,1)} %bitcast.88) | data formatting | bytes 67108864 | tf_op jit(solution)/shard_map/reshape | solution.py:75
  607.3 17.2 %fusion.12 = f32[2,8,256,512]{2,1,0,3:T(8,128)} fusion(bf16[256,2,64,512,1]{0,2,1,4,3:T(8,128)(2,1)} %copy.18, bf16[2,8,2,64,512]{3,1,2,0,4:T(8,128)(2,1)} %copy.15), kind=kOutput, calls=%fused_computation.29 | convolution fusion | flops 538968064 | bytes 44040192 | tf_op jit(solution)/shard_map/riptc,jptc->rijc/dot_general | solution.py:33
  624.5 9.9 %copy.16 = f32[2,8,256,512]{3,2,1,0:T(8,128)} copy(f32[2,8,256,512]{2,1,0,3:T(8,128)} %fusion.12) | data formatting | bytes 16777216 | tf_op jit(solution)/shard_map/mul | solution.py:36
  (5 shorter events, 0.0 us)
Async XLA Ops:
  6.5 550.0 %all-gather.2.cloned.1.call-start = ((), (), s32[]{:S(2)}) async-start(), calls=%async_computation.1 | async-start | bytes 34603008 | tf_op jit(solution)/shard_map/all_gather | solution.py:74
  8.5 179.5 %collective-permute-start = (bf16[8,7,4096]{2,1,0:T(8,128)(2,1)S(1)}, bf16[8,7,4096]{2,1,0:T(8,128)(2,1)}, u32[]{:S(2)}, u32[]{:S(2)}) collective-permute-start(bf16[8,7,4096]{2,1,0:T(8,128)(2,1)S(1)} %slice.73), channel_id=1, source_target_pairs={{0,32},{32,64},{64,96},{1,33},{33,65},{65,97},{2,34},{34,66},{66,9... | collective-permute-start | bytes 1376264 | tf_op jit(solution)/shard_map/ppermute | solution.py:16
  10.6 33.0 %copy-start.6 = (f32[8,4096]{1,0:T(8,128)S(1)}, f32[8,4096]{1,0:T(8,128)}, u32[]{:S(2)}) copy-start(f32[8,4096]{1,0:T(8,128)} %param.3) | copy-start | bytes 393220
  158.1 13.7 %copy-start = (f32[4096,512]{0,1:T(8,128)S(1)}, f32[4096,512]{0,1:T(8,128)}, u32[]{:S(2)}) copy-start(f32[4096,512]{0,1:T(8,128)} %get-tuple-element.15) | copy-start | bytes 25165828
  158.1 16.5 %copy-start.1 = (f32[4096,512]{0,1:T(8,128)S(1)}, f32[4096,512]{0,1:T(8,128)}, u32[]{:S(2)}) copy-start(f32[4096,512]{0,1:T(8,128)} %get-tuple-element.16) | copy-start | bytes 25165828
  187.9 28.0 %slice-start = ((s8[16777216]{0:T(1024)(128)(4,1)}), s8[4194304]{0:T(1024)(128)(4,1)S(1)}, s32[]{:S(2)}) async-start(s8[16777216]{0:T(1024)(128)(4,1)} %bitcast.90), calls=%async_computation.2 | async-start | bytes 8388608
  193.6 22.3 %copy-start.2 = (f32[8,16,4096]{2,1,0:T(8,128)}, f32[8,16,4096]{2,1,0:T(8,128)S(1)}, u32[]{:S(2)}) copy-start(f32[8,16,4096]{2,1,0:T(8,128)S(1)} %multiply_add_fusion) | copy-start | bytes 6291460
  193.6 22.3 %slice-start.1 = ((s8[16777216]{0:T(1024)(128)(4,1)}), s8[4194304]{0:T(1024)(128)(4,1)S(1)}, s32[]{:S(2)}) async-start(s8[16777216]{0:T(1024)(128)(4,1)} %bitcast.90), calls=%async_computation.3 | async-start | bytes 8388608
  193.6 22.3 %slice-start.2 = ((s8[16777216]{0:T(1024)(128)(4,1)}), s8[4194304]{0:T(1024)(128)(4,1)S(1)}, s32[]{:S(2)}) async-start(s8[16777216]{0:T(1024)(128)(4,1)} %bitcast.90), calls=%async_computation.4 | async-start | bytes 8388608
  193.6 22.3 %slice-start.3 = ((s8[16777216]{0:T(1024)(128)(4,1)}), s8[4194304]{0:T(1024)(128)(4,1)S(1)}, s32[]{:S(2)}) async-start(s8[16777216]{0:T(1024)(128)(4,1)} %bitcast.90), calls=%async_computation.5 | async-start | bytes 8388608
  216.0 20.2 %copy-start.3 = (f32[8,16,4096]{2,1,0:T(8,128)S(1)}, f32[8,16,4096]{2,1,0:T(8,128)}, u32[]{:S(2)}) copy-start(f32[8,16,4096]{2,1,0:T(8,128)} %copy-done.2) | copy-start | bytes 6291460
  216.0 41.0 %slice-start.4 = ((s8[16777216]{0:T(1024)(128)(4,1)}), s8[4194304]{0:T(1024)(128)(4,1)S(1)}, s32[]{:S(2)}) async-start(s8[16777216]{0:T(1024)(128)(4,1)} %bitcast.94), calls=%async_computation.6 | async-start | bytes 8388608
  216.0 41.0 %slice-start.5 = ((s8[16777216]{0:T(1024)(128)(4,1)}), s8[4194304]{0:T(1024)(128)(4,1)S(1)}, s32[]{:S(2)}) async-start(s8[16777216]{0:T(1024)(128)(4,1)} %bitcast.94), calls=%async_computation.7 | async-start | bytes 8388608
  236.2 20.8 %slice-start.6 = ((s8[16777216]{0:T(1024)(128)(4,1)}), s8[4194304]{0:T(1024)(128)(4,1)S(1)}, s32[]{:S(2)}) async-start(s8[16777216]{0:T(1024)(128)(4,1)} %bitcast.94), calls=%async_computation.8 | async-start | bytes 8388608
  236.2 20.8 %slice-start.7 = ((s8[16777216]{0:T(1024)(128)(4,1)}), s8[4194304]{0:T(1024)(128)(4,1)S(1)}, s32[]{:S(2)}) async-start(s8[16777216]{0:T(1024)(128)(4,1)} %bitcast.94), calls=%async_computation.9 | async-start | bytes 8388608
  257.0 17.6 %copy-start.4 = (bf16[1,8,16,2,512]{4,2,3,1,0:T(8,128)(2,1)S(1)}, bf16[1,8,16,2,512]{4,2,3,1,0:T(8,128)(2,1)}, u32[]{:S(2)}) copy-start(bf16[1,8,16,2,512]{4,2,3,1,0:T(8,128)(2,1)} %fusion.45) | copy-start | bytes 786436
  257.0 17.6 %copy-start.5 = (bf16[1,8,16,2,512]{4,2,3,1,0:T(8,128)(2,1)S(1)}, bf16[1,8,16,2,512]{4,2,3,1,0:T(8,128)(2,1)}, u32[]{:S(2)}) copy-start(bf16[1,8,16,2,512]{4,2,3,1,0:T(8,128)(2,1)} %fusion.48) | copy-start | bytes 786436
Sparse Core Ops, SparseCore 0:
  293.5 263.0 all-gather.1
